TPU v7x, 512 devices: a whole 4x4x16 slice. The times are simulated.
512 devices in a mesh: seq: 32 (over z, core), dp: 4 (over x), tensor: 4 (over y).
Axes of the slice: x: 4, y: 4, z: 16, core: 2. Of those that a mesh axis runs over, the one named last changes fastest.
Arguments:
- attention_queries: bfloat16 [4, 4096, 3584], P('dp', 'seq', 'tensor')
- attention_keys: bfloat16 [4, 4096, 512], P('dp', 'seq', 'tensor')
- attention_values: bfloat16 [4, 4096, 512], P('dp', 'seq', 'tensor')
- key_window_length: int32 [4], P('tensor'), may hold values from 128 to 512, as said below
- norm_gain: float32 [3584], P('tensor'), may hold values from 0.5 to 2
- spike_levels: int32 [3584], P('tensor'), may hold values from 1 to 4
- lin_queries: bfloat16 [4, 4096, 3584], P('dp', 'seq', 'tensor'), may hold values from -6 to 6
- lin_keys: bfloat16 [4, 4096, 3584], P('dp', 'seq', 'tensor'), may hold values from -6 to 6
- decay_logs: float32 [4, 28, 4096], P('dp', 'tensor', 'seq'), as said below
- cotangent: bfloat16 [4, 4096, 3584], P('dp', 'seq', 'tensor')
Outputs:
- layer_output: bfloat16 [4, 4096, 3584], P('dp', 'seq', 'tensor')
- query_grads: bfloat16 [4, 4096, 3584], P('dp', 'seq', 'tensor')
- key_gradient: bfloat16 [4, 4096, 512], P('dp', 'seq', 'tensor')
- value_gradient: bfloat16 [4, 4096, 512], P('dp', 'seq', 'tensor')
- gain_grads: float32 [3584], P('tensor')
Inputs may be any that keep to these rules, and one draw needn't show every extreme that they name: Key head g lets query t see positions j with t - key_window_length[g] < j <= t; some head has exactly 512. `decay_logs`: non-positive.
All inputs are finite; a program needn't handle non-finite values.
Results may differ from a plain program's by a relative error of at most 0.015.
Values may be sent and summed in bfloat16 or wider, within the bound.
No kernel may reach another device: no remote copies, remote signals or barrier semaphores. Data moves between devices by JAX's collectives and lax.ppermute only.
A program may use at most 128 MiB of HBM per device.

v0:
```python
import math
import jax
import jax.numpy as jnp
from jax import lax
from jax.sharding import PartitionSpec as P

HEAD_SIZE = 128
D = 3584
LONGEST_WINDOW = 512
precise = lax.Precision.HIGHEST
epsilon = 1e-06


def passed_along(block, axis, distance):
    devices = range(lax.axis_size(axis))
    route = [(i - distance, i) for i in devices if i - distance in devices]
    return lax.ppermute(block, axis, route)


def entering(value, axis, join, neutral, backward):
    count, mine = (lax.axis_size(axis), lax.axis_index(axis))
    pieces = jax.tree.map(lambda part: lax.all_gather(part, axis), value)
    if backward:
        pieces = jax.tree.map(lambda part: part[::-1], pieces)
        mine = count - 1 - mine
    running = jax.tree.map(
        lambda part, zero: jnp.full_like(part, 0) + jnp.asarray(zero, part.dtype), value, neutral
    )

    def turn(position, running):
        longer = join(running, jax.tree.map(lambda part: part[position], pieces))
        return jax.tree.map(lambda new, old: jnp.where(position < mine, new, old), longer, running)

    return lax.fori_loop(0, count - 1, turn, running)


def head_logits(query_rows, key_row_block, first_query, key_reach, scaling):
    block_rows = query_rows.shape[0]
    key_span = key_row_block.shape[0] - block_rows
    logits = (
        jnp.einsum("sd,kd->sk", query_rows, key_row_block, preferred_element_type=jnp.float32)
        * scaling
    )
    query_pos = first_query + jnp.arange(block_rows, dtype=jnp.int32)[:, None]
    key_pos = first_query - key_span + jnp.arange(key_row_block.shape[0], dtype=jnp.int32)[None, :]
    allowed = (key_pos >= 0) & (key_pos <= query_pos) & (key_pos > query_pos - key_reach)
    return jnp.where(allowed, logits, -jnp.inf)


def chain_states(earlier, later):
    return (earlier[0] * later[0], later[0][:, None, None] * earlier[1] + later[1])


def local(
    attention_queries,
    attention_keys,
    attention_values,
    key_window_length,
    norm_gain,
    spike_levels,
    lin_queries,
    lin_keys,
    decay_logs,
    cotangent,
):
    block_rows = attention_queries.shape[1]
    q_heads = attention_queries.shape[2] // HEAD_SIZE
    kv_heads = attention_keys.shape[2] // HEAD_SIZE
    head_groups = q_heads // kv_heads
    previous = (LONGEST_WINDOW + block_rows - 1) // block_rows
    key_span = previous * block_rows
    first_query = lax.axis_index("seq") * block_rows
    scaling = 1.0 / math.sqrt(HEAD_SIZE)
    own_pair = jnp.stack([attention_keys, attention_values])
    earlier_blocks = []
    moving = own_pair
    for distance in range(previous):
        moving = passed_along(moving, "seq", 1)
        earlier_blocks.append(moving)
    window_pair = jnp.concatenate(earlier_blocks[::-1] + [own_pair], axis=2)
    window_pair = window_pair.reshape(2, key_span + block_rows, kv_heads, HEAD_SIZE).transpose(
        0, 2, 1, 3
    )
    window_keys = window_pair[0]
    window_values = window_pair[1]
    head_queries = attention_queries[0].reshape(block_rows, q_heads, HEAD_SIZE).transpose(1, 0, 2)
    kv_of_head = jnp.arange(q_heads, dtype=jnp.int32) // head_groups

    def forward_head(operands):
        query_rows, kv_index = operands
        key_row_block = lax.dynamic_index_in_dim(window_keys, kv_index, 0, keepdims=False)
        value_rows = lax.dynamic_index_in_dim(window_values, kv_index, 0, keepdims=False)
        key_reach = lax.dynamic_index_in_dim(key_window_length, kv_index, 0, keepdims=False)
        logits = head_logits(query_rows, key_row_block, first_query, key_reach, scaling)
        row_max = jnp.max(logits, axis=-1)
        exponent = jnp.exp(logits - row_max[:, None])
        row_sum = jnp.sum(exponent, axis=-1)
        weights = (exponent / row_sum[:, None]).astype(jnp.bfloat16)
        head_output = jnp.dot(weights, value_rows, preferred_element_type=jnp.float32).astype(
            jnp.bfloat16
        )
        return (head_output, row_max, row_sum)

    heads_out, maxima, sums = lax.map(forward_head, (head_queries, kv_of_head))
    out_float = heads_out.astype(jnp.float32)
    square_sum = lax.psum(jnp.sum(out_float * out_float, axis=(0, 2)), "tensor")
    inverse = 1.0 / jnp.sqrt(square_sum / D + epsilon)
    normed = out_float * inverse[None, :, None]
    gain_rows = norm_gain.reshape(q_heads, HEAD_SIZE)[:, None, :]
    ceiling = spike_levels.astype(jnp.float32).reshape(q_heads, HEAD_SIZE)[:, None, :]
    bounded = jnp.tanh(normed * gain_rows / ceiling)
    spikes = (ceiling * bounded).astype(jnp.bfloat16)
    membrane_queries = lin_queries[0].reshape(block_rows, q_heads, HEAD_SIZE).transpose(1, 0, 2)
    membrane_keys = lin_keys[0].reshape(block_rows, q_heads, HEAD_SIZE).transpose(1, 0, 2)
    cumulative = jnp.cumsum(decay_logs[0], axis=1)
    lower_mask = jnp.arange(block_rows)[:, None] >= jnp.arange(block_rows)[None, :]
    gaps = jnp.where(lower_mask[None], cumulative[:, :, None] - cumulative[:, None, :], 0.0)
    products = jnp.einsum(
        "hsd,htd->hst", membrane_queries, membrane_keys, preferred_element_type=jnp.float32
    )
    decayed = jnp.where(lower_mask[None], jnp.exp(gaps), 0.0) * products
    spike_float = spikes.astype(jnp.float32)
    query_float = membrane_queries.astype(jnp.float32)
    key_float = membrane_keys.astype(jnp.float32)
    block_decay = jnp.exp(cumulative[:, -1])
    tail_decay = jnp.exp(cumulative[:, -1:] - cumulative)
    local_state = jnp.einsum(
        "hsd,hse->hde", key_float * tail_decay[..., None], spike_float, precision=precise
    )
    identity = (jnp.ones_like(block_decay), jnp.zeros_like(local_state))
    decay_before, state_in = entering(
        (block_decay, local_state), "seq", chain_states, identity, False
    )
    carried = jnp.einsum("hsd,hde->hse", query_float, state_in, precision=precise)
    membrane = (
        jnp.einsum("hst,htd->hsd", decayed, spike_float, precision=precise)
        + jnp.exp(cumulative)[..., None] * carried
    )
    scale_out = 1.0 / jnp.sqrt(jnp.mean(membrane * membrane, axis=-1) + epsilon)
    unit_out = membrane * scale_out[..., None]
    layer_output = (
        unit_out.astype(jnp.bfloat16).transpose(1, 0, 2).reshape(1, block_rows, q_heads * HEAD_SIZE)
    )
    incoming = (
        cotangent[0].reshape(block_rows, q_heads, HEAD_SIZE).transpose(1, 0, 2).astype(jnp.float32)
    )
    membrane_grad = scale_out[..., None] * (
        incoming - unit_out * jnp.mean(incoming * unit_out, axis=-1, keepdims=True)
    )
    head_part = jnp.einsum(
        "hsd,hse->hde",
        query_float * jnp.exp(cumulative)[..., None],
        membrane_grad,
        precision=precise,
    )
    decay_after, state_after = entering(
        (block_decay, head_part), "seq", chain_states, identity, True
    )
    later_part = jnp.einsum("htd,hde->hte", key_float, state_after, precision=precise)
    spike_grad = (
        jnp.einsum("hst,hsd->htd", decayed, membrane_grad, precision=precise)
        + tail_decay[..., None] * later_part
    )
    level_grad = spike_grad * (1.0 - bounded * bounded)
    gain_part = jnp.sum(level_grad * normed, axis=1).reshape(q_heads * HEAD_SIZE)
    gain_grads = lax.psum(gain_part, ("seq", "dp"))
    normed_grad = level_grad * gain_rows
    slope_sum = lax.psum(jnp.sum(normed_grad * normed, axis=(0, 2)), "tensor")
    output_gradient = (
        inverse[None, :, None] * (normed_grad - normed * (slope_sum / D)[None, :, None])
    ).astype(jnp.bfloat16)

    def backward_head(operands):
        query_rows, grad_rows, row_max, row_sum, kv_index = operands
        key_row_block = lax.dynamic_index_in_dim(window_keys, kv_index, 0, keepdims=False)
        value_rows = lax.dynamic_index_in_dim(window_values, kv_index, 0, keepdims=False)
        key_reach = lax.dynamic_index_in_dim(key_window_length, kv_index, 0, keepdims=False)
        logits = head_logits(query_rows, key_row_block, first_query, key_reach, scaling)
        probs = jnp.exp(logits - row_max[:, None]) / row_sum[:, None]
        weights = probs.astype(jnp.bfloat16)
        prob_grad = jnp.einsum(
            "sd,kd->sk", grad_rows, value_rows, preferred_element_type=jnp.float32
        )
        row_delta = jnp.sum(probs * prob_grad, axis=-1, keepdims=True)
        logit_grad = (probs * (prob_grad - row_delta) * scaling).astype(jnp.bfloat16)
        query_grad = jnp.dot(logit_grad, key_row_block, preferred_element_type=jnp.float32)
        key_part = jnp.einsum(
            "sk,sd->kd", logit_grad, query_rows, preferred_element_type=jnp.float32
        )
        value_part = jnp.einsum("sk,sd->kd", weights, grad_rows, preferred_element_type=jnp.float32)
        return (query_grad, key_part, value_part)

    query_parts, key_parts, value_parts = lax.map(
        backward_head, (head_queries, output_gradient, maxima, sums, kv_of_head)
    )
    key_sum = key_parts.reshape(kv_heads, head_groups, key_span + block_rows, HEAD_SIZE).sum(axis=1)
    value_sum = value_parts.reshape(kv_heads, head_groups, key_span + block_rows, HEAD_SIZE).sum(
        axis=1
    )
    pair_grads = jnp.stack([key_sum, value_sum])
    own_grads = pair_grads[:, :, key_span:]
    carried_grads = jnp.zeros_like(own_grads)
    for distance in range(previous, 0, -1):
        offset = (previous - distance) * block_rows
        carried_grads = passed_along(
            carried_grads + pair_grads[:, :, offset : offset + block_rows], "seq", -1
        )
    total_grads = own_grads + carried_grads
    query_grads = (
        query_parts.astype(jnp.bfloat16)
        .transpose(1, 0, 2)
        .reshape(1, block_rows, q_heads * HEAD_SIZE)
    )
    key_gradient = (
        total_grads[0]
        .astype(jnp.bfloat16)
        .transpose(1, 0, 2)
        .reshape(1, block_rows, kv_heads * HEAD_SIZE)
    )
    value_gradient = (
        total_grads[1]
        .astype(jnp.bfloat16)
        .transpose(1, 0, 2)
        .reshape(1, block_rows, kv_heads * HEAD_SIZE)
    )
    return (layer_output, query_grads, key_gradient, value_gradient, gain_grads)


def solution(mesh):
    placed = (
        P("dp", "seq", "tensor"),
        P("dp", "seq", "tensor"),
        P("dp", "seq", "tensor"),
        P("tensor"),
        P("tensor"),
        P("tensor"),
        P("dp", "seq", "tensor"),
        P("dp", "seq", "tensor"),
        P("dp", "tensor", "seq"),
        P("dp", "seq", "tensor"),
    )
    return jax.shard_map(
        local,
        mesh=mesh,
        in_specs=placed,
        out_specs=(
            P("dp", "seq", "tensor"),
            P("dp", "seq", "tensor"),
            P("dp", "seq", "tensor"),
            P("dp", "seq", "tensor"),
            P("tensor"),
        ),
        check_vma=False,
    )
```

profile of v0, /device:TPU:128, one launch (start us, length us, event | category | flops | bytes accessed | tf_op | source)
XLA Modules:
  0.0 720.5 jit_solution(11965284962167923408)
XLA Ops:
  8.0 1.9 collective-permute-start
  10.9 3.9 collective-permute-done
  14.8 1.9 collective-permute-start.1
  16.9 4.7 collective-permute-done.1
  21.6 1.9 collective-permute-start.2
  23.6 4.8 collective-permute-done.2
  28.3 1.9 collective-permute-start.3
  33.4 1.8 collective-permute-done.3
  36.0 28.6 %while.62 = (s32[]{:T(128)}, bf16[7,128,128]{2,1,0:T(8,128)(2,1)S(1)}, f32[7,128]{1,0:T(8,128)}, f32[7,128]{1,0:T(8,128)}, s32[]{:T(128)}, /*index=5*/s32[]{:T(1...) while((s32[]{:T(128)}, ...), condition=%wide.region_4.5_spmd, body=%wide.region_1.4_spmd.sunk | while | flops 42944384 | bytes 1391389 | solution.py:104
  37.5 1.3 dynamic_update_slice.52
  38.8 1.3 dynamic_update_slice.51
  41.6 1.3 dynamic_update_slice.52
  45.7 1.3 dynamic_update_slice.52
  49.8 1.3 dynamic_update_slice.52
  51.1 1.3 dynamic_update_slice.51
  53.9 1.3 dynamic_update_slice.52
  57.9 1.3 dynamic_update_slice.52
  59.2 1.3 dynamic_update_slice.51
  62.0 1.3 dynamic_update_slice.52
  64.8 10.9 %psum.21 = f32[128]{0:T(128)S(1)} all-reduce(f32[128]{0:T(128)S(1)} %fusion.52), channel_id=1, replica_groups=mesh['seq'=32,'dp'=4,'tensor'=4] {'tensor'}, use_global_device_ids=true, to_apply=%region_6.7 | all-reduce | flops 128 | bytes 1024 | tf_op jit(solution)/shard_map/psum | solution.py:106
  79.2 50.1 %all-reduce = f32[224]{0:T(256)S(1)} all-reduce(f32[224]{0:T(256)S(1)} %dynamic-update-slice), channel_id=2, replica_groups=mesh['seq'=32,'dp'=4,'tensor'=4] {'seq'}, use_global_device_ids=true, to_apply=%add | all-reduce | flops 224 | bytes 1792
  130.1 41.7 %all-gather.6.cloned.1.call-done = f32[224,128,128]{2,1,0:T(8,128)} async-done(((f32[7,128,128]{2,1,0:T(8,128)}), f32[224,128,128]{2,1,0:T(8,128)}) %all-gather.6.cloned.1.call-update) | async-done | bytes 14680080 | tf_op jit(solution)/shard_map/all_gather | solution.py:22
  171.8 36.8 %while.64 = (s32[]{:T(128)}, f32[7,128,128]{2,1,0:T(8,128)S(1)}, s32[]{:T(128)}, f32[32,7]{1,0:T(8,128)S(1)}, f32[32,7,128,128]{3,2,1,0:T(8,128)}, /*index=5*/s32[]{:T(128)}, s32[]{:T(128)}) while((s32[]{:T(128)}, f32[7,128,128]{2,1,0:T(8,128)S(1)}, s32[]{:T(128)}, f32[32,7]{1,0:T(8,128)S(1)}, f32[32,7,128,128]{3,2,1,0:T(8,128)}, ...), condition=%wide.region_8.9_spmd.clone, body=%wide.region_7.8_spmd.clone.sunk | while | flops 458756 | bytes 1376453 | solution.py:34
  210.0 1.5 multiply_reduce_fusion.2
  211.6 1.9 fusion.56
  214.1 93.6 %all-gather.8.cloned.1.call-done = f32[224,128,128]{2,1,0:T(8,128)} async-done(((f32[7,128,128]{2,1,0:T(8,128)}), f32[224,128,128]{2,1,0:T(8,128)}) %all-gather.8.cloned.1.call-update) | async-done | bytes 14680080 | tf_op jit(solution)/shard_map/all_gather | solution.py:22
  307.7 13.1 %rev.7 = f32[32,7,128,128]{3,2,1,0:T(8,128)} reverse(f32[32,7,128,128]{3,2,1,0:T(8,128)} %bitcast.189), dimensions={0} | reverse | bytes 29360128 | tf_op jit(solution)/shard_map/rev | solution.py:24
  320.8 57.7 %while.65 = (s32[]{:T(128)}, f32[7,128,128]{2,1,0:T(8,128)S(1)}, s32[]{:T(128)}, f32[32,7]{1,0:T(8,128)}, f32[32,7,128,128]{3,2,1,0:T(8,128)}, /*index=5*/s32[]{:T(128)}, s32[]{:T(128)}) while((s32[]{:T(128)}, f32[7,128,128]{2,1,0:T(8,128)S(1)}, s32[]{:T(128)}, f32[32,7]{1,0:T(8,128)}, f32[32,7,128,128]{3,2,1,0:T(8,128)}, ...), condition=%wide.region_12.13_spmd.clone, body=%wide.region_11.12_spmd.clone.sunk | while | flops 458756 | bytes 1376453 | solution.py:34
  378.5 1.4 fusion.40
  379.9 3.7 fusion.51
  383.5 10.4 %psum.22 = f32[128]{0:T(128)S(1)} all-reduce(f32[128]{0:T(128)S(1)} %get-tuple-element.606), channel_id=1, replica_groups=mesh['seq'=32,'dp'=4,'tensor'=4] {'tensor'}, use_global_device_ids=true, to_apply=%region_14.15 | all-reduce | flops 128 | bytes 1024 | tf_op jit(solution)/shard_map/psum | solution.py:168
  395.2 39.9 %while.63 = (s32[]{:T(128)}, bf16[7,128,128]{1,2,0:T(8,128)(2,1)}, f32[7,640,128]{2,1,0:T(8,128)}, f32[7,640,128]{2,1,0:T(8,128)S(1)}, s32[]{:T(128)}, /*index=5...) while((s32[]{:T(128)}, bf16[7,128,128]{1,2,0:T(8,128)(2,1)}, ...), condition=%wide.region_17.18_spmd, body=%wide.region_15.17_spmd.sunk | while | flops 106088448 | bytes 3815853 | solution.py:193
  399.2 1.7 fusion.121
  404.9 1.8 fusion.121
  410.6 1.7 fusion.121
  416.4 1.7 fusion.121
  422.1 1.7 fusion.121
  427.7 1.7 fusion.121
  433.4 1.7 fusion.121
  435.3 1.8 reduce_sum.91
  437.2 2.1 collective-permute-start.4
  439.2 2.5 collective-permute-done.4
  441.7 5.0 collective-permute-start.5
  446.7 2.5 collective-permute-done.5
  449.2 5.0 collective-permute-start.6
  454.2 2.5 collective-permute-done.6
  456.8 5.0 collective-permute-start.7
  463.5 249.5 %psum.23 = f32[896]{0:T(1024)} all-reduce(f32[896]{0:T(1024)S(1)} %bitcast.224), channel_id=1, replica_groups=mesh['seq'=32,'dp'=4,'tensor'=4] {'seq','dp'}, use_global_device_ids=true, to_apply=%region_21.22 | all-reduce | flops 896 | bytes 7168 | tf_op jit(solution)/shard_map/psum | solution.py:166
  (323 shorter events, 151.2 us)
Async XLA Ops:
  7.2 164.7 %all-gather.6.cloned.1.call-start = ((), (), s32[]{:S(2)}) async-start(), calls=%async_computation | async-start | bytes 15138816 | tf_op jit(solution)/shard_map/all_gather | solution.py:22
  8.0 6.8 collective-permute-start
  14.8 6.8 collective-permute-start.1
  21.6 6.8 collective-permute-start.2
  23.5 52.1 %copy-start.11 = (f32[7,128]{1,0:T(8,128)}, f32[7,128]{1,0:T(8,128)S(1)}, u32[]{:S(2)}) copy-start(f32[7,128]{1,0:T(8,128)S(1)} %get-tuple-element.695) | copy-start | bytes 10756
  28.3 6.8 collective-permute-start.3
  31.0 178.2 %copy-start.13 = (f32[7,128]{1,0:T(8,128)}, f32[7,128]{1,0:T(8,128)S(1)}, u32[]{:S(2)}) copy-start(f32[7,128]{1,0:T(8,128)S(1)} %convert_bitcast_fusion) | copy-start | bytes 10756
  33.4 96.4 %copy-start.5 = (bf16[1,128,896]{1,2,0:T(8,128)(2,1)}, bf16[1,128,896]{1,2,0:T(8,128)(2,1)S(1)}, u32[]{:S(2)}) copy-start(bf16[1,128,896]{1,2,0:T(8,128)(2,1)S(1)} %copy.51) | copy-start | bytes 688132
  36.0 39.6 %copy-start.12 = (f32[896]{0:T(1024)S(1)}, f32[896]{0:T(1024)}, u32[]{:S(2)}) copy-start(f32[896]{0:T(1024)} %param.22) | copy-start | bytes 10756
  64.6 64.8 %copy-start.6 = (bf16[7,128,128]{2,1,0:T(8,128)(2,1)}, bf16[7,128,128]{2,1,0:T(8,128)(2,1)S(1)}, u32[]{:S(2)}) copy-start(bf16[7,128,128]{2,1,0:T(8,128)(2,1)S(1)} %get-tuple-element.1047) | copy-start | bytes 688132
  64.6 144.6 %copy-start.3 = (bf16[7,128,128]{2,1,0:T(8,128)(2,1)}, bf16[7,128,128]{2,1,0:T(8,128)(2,1)S(1)}, u32[]{:S(2)}) copy-start(bf16[7,128,128]{2,1,0:T(8,128)(2,1)S(1)} %get-tuple-element.500) | copy-start | bytes 688132
  64.6 64.8 %copy-start.8 = (bf16[1,128,896]{2,1,0:T(8,128)(2,1)S(1)}, bf16[1,128,896]{2,1,0:T(8,128)(2,1)}, u32[]{:S(2)}) copy-start(bf16[1,128,896]{2,1,0:T(8,128)(2,1)} %param.24) | copy-start | bytes 688132
  64.6 65.0 %copy-start.10 = (bf16[1,128,896]{2,1,0:T(8,128)(2,1)S(1)}, bf16[1,128,896]{2,1,0:T(8,128)(2,1)}, u32[]{:S(2)}) copy-start(bf16[1,128,896]{2,1,0:T(8,128)(2,1)} %param.27) | copy-start | bytes 688132
  75.6 133.6 %copy-start.15 = (f32[128]{0:T(128)}, f32[128]{0:T(128)S(1)}, u32[]{:S(2)}) copy-start(f32[128]{0:T(128)S(1)} %add_rsqrt_fusion.1) | copy-start | bytes 1540
  77.0 230.7 %all-gather.8.cloned.1.call-start = ((), (), s32[]{:S(2)}) async-start(), calls=%async_computation.1 | async-start | bytes 15138816 | tf_op jit(solution)/shard_map/all_gather | solution.py:22
  130.1 79.1 %copy-start.16 = (f32[7,128,128]{2,1,0:T(8,128)}, f32[7,128,128]{2,1,0:T(8,128)S(1)}, u32[]{:S(2)}) copy-start(f32[7,128,128]{2,1,0:T(8,128)S(1)} %convolution_multiply_fusion.3) | copy-start | bytes 1376260
  209.2 0.8 copy-start
  211.5 2.6 copy-start.2
  379.9 14.1 %copy-start.4 = (bf16[7,128,128]{2,1,0:T(8,128)(2,1)S(1)}, bf16[7,128,128]{2,1,0:T(8,128)(2,1)}, u32[]{:S(2)}) copy-start(bf16[7,128,128]{2,1,0:T(8,128)(2,1)} %copy-done.3) | copy-start | bytes 688132
  437.1 24.7 %copy-start.1 = (f32[7,128,128]{2,1,0:T(8,128)S(1)}, f32[7,128,128]{2,1,0:T(8,128)}, u32[]{:S(2)}) copy-start(f32[7,128,128]{2,1,0:T(8,128)} %copy-done) | copy-start | bytes 1376260
  437.1 24.7 %copy-start.7 = (f32[7,128,128]{1,2,0:T(8,128)S(1)}, f32[7,128,128]{1,2,0:T(8,128)}, u32[]{:S(2)}) copy-start(f32[7,128,128]{1,2,0:T(8,128)} %get-tuple-element.696) | copy-start | bytes 1376260
  437.1 25.6 %copy-start.9 = (bf16[7,128,128]{1,2,0:T(8,128)(2,1)S(1)}, bf16[7,128,128]{1,2,0:T(8,128)(2,1)}, u32[]{:S(2)}) copy-start(bf16[7,128,128]{1,2,0:T(8,128)(2,1)} %get-tuple-element.505) | copy-start | bytes 688132
  437.1 26.4 %copy-start.14 = (f32[7,128]{1,0:T(8,128)S(1)}, f32[7,128]{1,0:T(8,128)}, u32[]{:S(2)}) copy-start(f32[7,128]{1,0:T(8,128)} %get-tuple-element.605) | copy-start | bytes 10756
  437.2 4.6 collective-permute-start.4
  441.7 7.5 %collective-permute-start.5 = (f32[2,1,128,128]{3,2,1,0:T(8,128)S(1)}, f32[2,1,128,128]{3,2,1,0:T(8,128)S(1)}, u32[]{:S(2)}, u32[]{:S(2)}) collective-permute-start(f32[2,1,128,128]{3,2,1,0:T(8,128)S(1)} %fusion.71), channel_id=1, source_target_pairs={{16,0},{32,16},{48,32},{64,48},{80,64},{96,80},{112,96},{128,112},... | collective-permute-start | bytes 393224 | tf_op jit(solution)/shard_map/ppermute | solution.py:17
  449.2 7.5 %collective-permute-start.6 = (f32[2,1,128,128]{3,2,1,0:T(8,128)S(1)}, f32[2,1,128,128]{3,2,1,0:T(8,128)S(1)}, u32[]{:S(2)}, u32[]{:S(2)}) collective-permute-start(f32[2,1,128,128]{3,2,1,0:T(8,128)S(1)} %fusion.65), channel_id=1, source_target_pairs={{16,0},{32,16},{48,32},{64,48},{80,64},{96,80},{112,96},{128,112},... | collective-permute-start | bytes 393224 | tf_op jit(solution)/shard_map/ppermute | solution.py:17
  456.8 256.3 %collective-permute-start.7 = (f32[2,1,128,128]{3,2,1,0:T(8,128)S(1)}, f32[2,1,128,128]{3,2,1,0:T(8,128)S(1)}, u32[]{:S(2)}, u32[]{:S(2)}) collective-permute-start(f32[2,1,128,128]{3,2,1,0:T(8,128)S(1)} %fusion.72), channel_id=1, source_target_pairs={{16,0},{32,16},{48,32},{64,48},{80,64},{96,80},{112,96},{128,112},... | collective-permute-start | bytes 393224 | tf_op jit(solution)/shard_map/ppermute | solution.py:17
Sparse Core Ops, SparseCore 0:
  77.1 94.7 all-gather.5
  213.6 94.0 all-gather.7
where the time goes:
time: 727 us; the launch traced here: 721 us
  blocking collectives  321 us (44%)
  waiting for transfers between devices  158 us (22%)
  other arithmetic  88.5 us (12%)
  local copies, waits for them, and re-layouts  67 us (9%)
  matrix products  44.1 us (6%)
  starting transfers between devices  24.7 us (3%)
  between operations  15.1 us (2%)
    psum x1, blocking collectives, local(): gain_grads = lax.psum(gain_part, ('seq', 'dp'))  250 us
    all_gather x2, waiting for transfers between devices, entering(): pieces = jax.tree.map(lambda part: lax.all_gather(part, axis), value)  135 us
    select_n x62, other arithmetic, turn(): jnp.where(position < mine, new, old)  70.8 us
    unnamed x1, blocking collectives  50.1 us
    ppermute x8, starting transfers between devices, passed_along(): return lax.ppermute(block, axis, route)  24.7 us
    ppermute x8, waiting for transfers between devices, passed_along(): return lax.ppermute(block, axis, route)  22.6 us
    mul x62, local copies, waits for them, and re-layouts, chain_states(): later[0][:, None, None] * earlier[1] + later[1]  21.9 us
    dynamic_update_slice x14, local copies, waits for them, and re-layouts, local(): heads_out, maxima, sums = lax.map(forward_head, (head_queries, kv_of_head))  18.1 us
  transfers between devices with their start and end apart: 10, of which 9 were waited for; matrix products, arithmetic and copies ran while one was open for 1% of the time, Pallas kernels for 0%

commit v1 on v0

--- a/solution.py
+++ b/solution.py
@@ -163,7 +163,7 @@
     )
     level_grad = spike_grad * (1.0 - bounded * bounded)
     gain_part = jnp.sum(level_grad * normed, axis=1).reshape(q_heads * HEAD_SIZE)
-    gain_grads = lax.psum(gain_part, ("seq", "dp"))
+    gain_grads = jnp.sum(lax.all_gather(gain_part, ("seq", "dp")), axis=0)
     normed_grad = level_grad * gain_rows
     slope_sum = lax.psum(jnp.sum(normed_grad * normed, axis=(0, 2)), "tensor")
     output_gradient = (

time: 727 us -> 621 us (0.85)
  the two profiles are of different devices: /device:TPU:128 before, /device:TPU:97 now
where the time goes in v1:
time: 621 us; the launch traced here: 615 us
  blocking collectives  210 us (34%)
  waiting for transfers between devices  155 us (25%)
  other arithmetic  89.5 us (14%)
  local copies, waits for them, and re-layouts  67 us (11%)
  matrix products  44.1 us (7%)
  starting transfers between devices  32 us (5%)
  between operations  15.1 us (2%)
    all_gather x1, blocking collectives, local(): gain_grads = jnp.sum(lax.all_gather(gain_part, ('seq', 'dp')), axis=0)  142 us
    all_gather x2, waiting for transfers between devices, entering(): pieces = jax.tree.map(lambda part: lax.all_gather(part, axis), value)  137 us
    select_n x62, other arithmetic, turn(): jnp.where(position < mine, new, old)  70.8 us
    unnamed x1, blocking collectives  50.3 us
    ppermute x8, starting transfers between devices, passed_along(): return lax.ppermute(block, axis, route)  31.9 us
    mul x62, local copies, waits for them, and re-layouts, chain_states(): later[0][:, None, None] * earlier[1] + later[1]  21.9 us
    dynamic_update_slice x14, local copies, waits for them, and re-layouts, local(): heads_out, maxima, sums = lax.map(forward_head, (head_queries, kv_of_head))  18.1 us
    ppermute x8, waiting for transfers between devices, passed_along(): return lax.ppermute(block, axis, route)  17.6 us
  transfers between devices with their start and end apart: 10, of which 8 were waited for; matrix products, arithmetic and copies ran while one was open for 2% of the time, Pallas kernels for 0%

profile of v1, /device:TPU:97, one launch (start us, length us, event | category | flops | bytes accessed | tf_op | source)
XLA Modules:
  0.0 614.7 jit_solution(16341887338407245856)
XLA Ops:
  8.0 5.3 collective-permute-start
  14.6 5.5 collective-permute-start.1
  21.4 5.5 collective-permute-start.2
  28.2 5.5 collective-permute-start.3
  37.7 28.6 %while.62 = (s32[]{:T(128)}, bf16[7,128,128]{2,1,0:T(8,128)(2,1)S(1)}, f32[7,128]{1,0:T(8,128)}, f32[7,128]{1,0:T(8,128)}, s32[]{:T(128)}, /*index=5*/s32[]{:T(1...) while((s32[]{:T(128)}, ...), condition=%wide.region_4.5_spmd, body=%wide.region_1.4_spmd.sunk | while | flops 42944384 | bytes 1391389 | solution.py:104
  39.2 1.3 dynamic_update_slice.52
  40.5 1.3 dynamic_update_slice.51
  43.3 1.3 dynamic_update_slice.52
  44.6 1.3 dynamic_update_slice.51
  47.4 1.3 dynamic_update_slice.52
  48.7 1.3 dynamic_update_slice.51
  51.5 1.3 dynamic_update_slice.52
  52.8 1.3 dynamic_update_slice.51
  55.5 1.3 dynamic_update_slice.52
  56.8 1.3 dynamic_update_slice.51
  59.6 1.3 dynamic_update_slice.52
  60.9 1.3 dynamic_update_slice.51
  63.7 1.3 dynamic_update_slice.52
  65.0 1.3 dynamic_update_slice.51
  66.4 8.9 %psum.14 = f32[128]{0:T(128)S(1)} all-reduce(f32[128]{0:T(128)S(1)} %fusion.52), channel_id=1, replica_groups=mesh['seq'=32,'dp'=4,'tensor'=4] {'tensor'}, use_global_device_ids=true, to_apply=%region_6.7 | all-reduce | flops 128 | bytes 1024 | tf_op jit(solution)/shard_map/psum | solution.py:106
  78.9 50.3 %all-reduce = f32[224]{0:T(256)S(1)} all-reduce(f32[224]{0:T(256)S(1)} %dynamic-update-slice), channel_id=2, replica_groups=mesh['seq'=32,'dp'=4,'tensor'=4] {'seq'}, use_global_device_ids=true, to_apply=%add | all-reduce | flops 224 | bytes 1792
  130.0 43.8 %all-gather.7.cloned.1.call-done = f32[224,128,128]{2,1,0:T(8,128)} async-done(((f32[7,128,128]{2,1,0:T(8,128)}), f32[224,128,128]{2,1,0:T(8,128)}) %all-gather.7.cloned.1.call-update) | async-done | bytes 14680080 | tf_op jit(solution)/shard_map/all_gather | solution.py:22
  173.8 36.8 %while.64 = (s32[]{:T(128)}, f32[7,128,128]{2,1,0:T(8,128)S(1)}, s32[]{:T(128)}, f32[32,7]{1,0:T(8,128)S(1)}, f32[32,7,128,128]{3,2,1,0:T(8,128)}, /*index=5*/s32[]{:T(128)}, s32[]{:T(128)}) while((s32[]{:T(128)}, f32[7,128,128]{2,1,0:T(8,128)S(1)}, s32[]{:T(128)}, f32[32,7]{1,0:T(8,128)S(1)}, f32[32,7,128,128]{3,2,1,0:T(8,128)}, ...), condition=%wide.region_8.9_spmd.clone, body=%wide.region_7.8_spmd.clone.sunk | while | flops 458756 | bytes 1376453 | solution.py:34
  211.9 1.5 multiply_reduce_fusion.2
  213.6 1.9 fusion.56
  216.1 93.6 %all-gather.9.cloned.1.call-done = f32[224,128,128]{2,1,0:T(8,128)} async-done(((f32[7,128,128]{2,1,0:T(8,128)}), f32[224,128,128]{2,1,0:T(8,128)}) %all-gather.9.cloned.1.call-update) | async-done | bytes 14680080 | tf_op jit(solution)/shard_map/all_gather | solution.py:22
  309.7 13.1 %rev.7 = f32[32,7,128,128]{3,2,1,0:T(8,128)} reverse(f32[32,7,128,128]{3,2,1,0:T(8,128)} %bitcast.188), dimensions={0} | reverse | bytes 29360128 | tf_op jit(solution)/shard_map/rev | solution.py:24
  322.8 57.7 %while.65 = (s32[]{:T(128)}, f32[7,128,128]{2,1,0:T(8,128)S(1)}, s32[]{:T(128)}, f32[32,7]{1,0:T(8,128)}, f32[32,7,128,128]{3,2,1,0:T(8,128)}, /*index=5*/s32[]{:T(128)}, s32[]{:T(128)}) while((s32[]{:T(128)}, f32[7,128,128]{2,1,0:T(8,128)S(1)}, s32[]{:T(128)}, f32[32,7]{1,0:T(8,128)}, f32[32,7,128,128]{3,2,1,0:T(8,128)}, ...), condition=%wide.region_12.13_spmd.clone, body=%wide.region_11.12_spmd.clone.sunk | while | flops 458756 | bytes 1376453 | solution.py:34
  380.4 1.4 fusion.40
  381.8 3.7 fusion.51
  385.5 8.4 %psum.15 = f32[128]{0:T(128)S(1)} all-reduce(f32[128]{0:T(128)S(1)} %get-tuple-element.606), channel_id=1, replica_groups=mesh['seq'=32,'dp'=4,'tensor'=4] {'tensor'}, use_global_device_ids=true, to_apply=%region_14.15 | all-reduce | flops 128 | bytes 1024 | tf_op jit(solution)/shard_map/psum | solution.py:168
  395.2 39.9 %while.63 = (s32[]{:T(128)}, bf16[7,128,128]{1,2,0:T(8,128)(2,1)}, f32[7,640,128]{2,1,0:T(8,128)}, f32[7,640,128]{2,1,0:T(8,128)S(1)}, s32[]{:T(128)}, /*index=5...) while((s32[]{:T(128)}, bf16[7,128,128]{1,2,0:T(8,128)(2,1)}, ...), condition=%wide.region_17.18_spmd, body=%wide.region_15.17_spmd.sunk | while | flops 106088448 | bytes 3815853 | solution.py:193
  399.1 1.7 fusion.121
  404.9 1.8 fusion.121
  410.6 1.7 fusion.121
  416.3 1.7 fusion.121
  422.0 1.7 fusion.121
  427.7 1.7 fusion.121
  433.4 1.7 fusion.121
  435.2 1.8 reduce_sum.100
  437.1 4.3 collective-permute-start.4
  441.4 3.8 collective-permute-done.4
  445.3 2.1 collective-permute-start.5
  447.3 5.6 collective-permute-done.5
  452.9 1.9 collective-permute-start.6
  454.8 5.6 collective-permute-done.6
  460.4 1.9 collective-permute-start.7
  463.3 142.1 %all-gather.3 = f32[128,1,896]{2,1,0:T(1,128)S(1)} all-gather(f32[1,1,896]{2,1,0:T(1,128)S(1)} %reshape.161), channel_id=1, replica_groups=mesh['seq'=32,'dp'=4,'tensor'=4] {'seq','dp'}, dimensions={0}, use_global_device_ids=true | all-gather | bytes 462336 | tf_op jit(solution)/shard_map/all_gather | solution.py:166
  (325 shorter events, 149.7 us)
Async XLA Ops:
  7.2 166.7 %all-gather.7.cloned.1.call-start = ((), (), s32[]{:S(2)}) async-start(), calls=%async_computation | async-start | bytes 15138816 | tf_op jit(solution)/shard_map/all_gather | solution.py:22
  8.0 6.6 %collective-permute-start = (bf16[2,1,128,128]{3,2,1,0:T(8,128)(2,1)S(1)}, bf16[2,1,128,128]{3,2,1,0:T(8,128)(2,1)S(1)}, u32[]{:S(2)}, u32[]{:S(2)}) collective-permute-start(bf16[2,1,128,128]{3,2,1,0:T(8,128)(2,1)S(1)} %pad_maximum_fusion.1), channel_id=1, source_target_pairs={{0,16},{16,32},{32,48},{48,64},{64,80},{80,96},{96,112},{112,128},... | collective-permute-start | bytes 196616 | tf_op jit(solution)/shard_map/ppermute | solution.py:17
  14.6 6.8 %collective-permute-start.1 = (bf16[2,1,128,128]{3,2,1,0:T(8,128)(2,1)S(1)}, bf16[2,1,128,128]{3,2,1,0:T(8,128)(2,1)S(1)}, u32[]{:S(2)}, u32[]{:S(2)}) collective-permute-start(bf16[2,1,128,128]{3,2,1,0:T(8,128)(2,1)S(1)} %collective-permute-done), channel_id=1, source_target_pairs={{0,16},{16,32},{32,48},{48,64},{64,80},{80,96},{96,112},{112,128},... | collective-permute-start | bytes 196616 | tf_op jit(solution)/shard_map/ppermute | solution.py:17
  21.4 6.8 %collective-permute-start.2 = (bf16[2,1,128,128]{3,2,1,0:T(8,128)(2,1)S(1)}, bf16[2,1,128,128]{3,2,1,0:T(8,128)(2,1)S(1)}, u32[]{:S(2)}, u32[]{:S(2)}) collective-permute-start(bf16[2,1,128,128]{3,2,1,0:T(8,128)(2,1)S(1)} %collective-permute-done.1), channel_id=1, source_target_pairs={{0,16},{16,32},{32,48},{48,64},{64,80},{80,96},{96,112},{112,128},... | collective-permute-start | bytes 196616 | tf_op jit(solution)/shard_map/ppermute | solution.py:17
  26.9 48.3 %copy-start.11 = (f32[7,128]{1,0:T(8,128)}, f32[7,128]{1,0:T(8,128)S(1)}, u32[]{:S(2)}) copy-start(f32[7,128]{1,0:T(8,128)S(1)} %get-tuple-element.695) | copy-start | bytes 10756
  28.2 8.6 %collective-permute-start.3 = (bf16[2,1,128,128]{3,2,1,0:T(8,128)(2,1)S(1)}, bf16[2,1,128,128]{3,2,1,0:T(8,128)(2,1)S(1)}, u32[]{:S(2)}, u32[]{:S(2)}) collective-permute-start(bf16[2,1,128,128]{3,2,1,0:T(8,128)(2,1)S(1)} %collective-permute-done.2), channel_id=1, source_target_pairs={{0,16},{16,32},{32,48},{48,64},{64,80},{80,96},{96,112},{112,128},... | collective-permute-start | bytes 196616 | tf_op jit(solution)/shard_map/ppermute | solution.py:17
  34.4 176.8 %copy-start.13 = (f32[7,128]{1,0:T(8,128)}, f32[7,128]{1,0:T(8,128)S(1)}, u32[]{:S(2)}) copy-start(f32[7,128]{1,0:T(8,128)S(1)} %convert_bitcast_fusion) | copy-start | bytes 10756
  36.8 92.9 %copy-start.5 = (bf16[1,128,896]{1,2,0:T(8,128)(2,1)}, bf16[1,128,896]{1,2,0:T(8,128)(2,1)S(1)}, u32[]{:S(2)}) copy-start(bf16[1,128,896]{1,2,0:T(8,128)(2,1)S(1)} %copy.51) | copy-start | bytes 688132
  37.7 37.6 %copy-start.12 = (f32[896]{0:T(1024)S(1)}, f32[896]{0:T(1024)}, u32[]{:S(2)}) copy-start(f32[896]{0:T(1024)} %param.22) | copy-start | bytes 10756
  66.3 63.0 %copy-start.6 = (bf16[7,128,128]{2,1,0:T(8,128)(2,1)}, bf16[7,128,128]{2,1,0:T(8,128)(2,1)S(1)}, u32[]{:S(2)}) copy-start(bf16[7,128,128]{2,1,0:T(8,128)(2,1)S(1)} %get-tuple-element.1047) | copy-start | bytes 688132
  66.3 144.9 %copy-start.3 = (bf16[7,128,128]{2,1,0:T(8,128)(2,1)}, bf16[7,128,128]{2,1,0:T(8,128)(2,1)S(1)}, u32[]{:S(2)}) copy-start(bf16[7,128,128]{2,1,0:T(8,128)(2,1)S(1)} %get-tuple-element.500) | copy-start | bytes 688132
  66.3 63.0 %copy-start.8 = (bf16[1,128,896]{2,1,0:T(8,128)(2,1)S(1)}, bf16[1,128,896]{2,1,0:T(8,128)(2,1)}, u32[]{:S(2)}) copy-start(bf16[1,128,896]{2,1,0:T(8,128)(2,1)} %param.24) | copy-start | bytes 688132
  66.3 63.2 %copy-start.10 = (bf16[1,128,896]{2,1,0:T(8,128)(2,1)S(1)}, bf16[1,128,896]{2,1,0:T(8,128)(2,1)}, u32[]{:S(2)}) copy-start(bf16[1,128,896]{2,1,0:T(8,128)(2,1)} %param.27) | copy-start | bytes 688132
  75.3 135.9 %copy-start.15 = (f32[128]{0:T(128)}, f32[128]{0:T(128)S(1)}, u32[]{:S(2)}) copy-start(f32[128]{0:T(128)S(1)} %add_rsqrt_fusion.1) | copy-start | bytes 1540
  76.6 233.0 %all-gather.9.cloned.1.call-start = ((), (), s32[]{:S(2)}) async-start(), calls=%async_computation.1 | async-start | bytes 15138816 | tf_op jit(solution)/shard_map/all_gather | solution.py:22
  130.0 81.2 %copy-start.16 = (f32[7,128,128]{2,1,0:T(8,128)}, f32[7,128,128]{2,1,0:T(8,128)S(1)}, u32[]{:S(2)}) copy-start(f32[7,128,128]{2,1,0:T(8,128)S(1)} %convolution_multiply_fusion.3) | copy-start | bytes 1376260
  211.2 0.8 copy-start
  213.5 2.6 copy-start.2
  381.8 12.1 %copy-start.4 = (bf16[7,128,128]{2,1,0:T(8,128)(2,1)S(1)}, bf16[7,128,128]{2,1,0:T(8,128)(2,1)}, u32[]{:S(2)}) copy-start(bf16[7,128,128]{2,1,0:T(8,128)(2,1)} %copy-done.3) | copy-start | bytes 688132
  437.0 25.3 %copy-start.1 = (f32[7,128,128]{2,1,0:T(8,128)S(1)}, f32[7,128,128]{2,1,0:T(8,128)}, u32[]{:S(2)}) copy-start(f32[7,128,128]{2,1,0:T(8,128)} %copy-done) | copy-start | bytes 1376260
  437.0 25.3 %copy-start.7 = (f32[7,128,128]{1,2,0:T(8,128)S(1)}, f32[7,128,128]{1,2,0:T(8,128)}, u32[]{:S(2)}) copy-start(f32[7,128,128]{1,2,0:T(8,128)} %get-tuple-element.696) | copy-start | bytes 1376260
  437.1 26.2 %copy-start.14 = (f32[7,128]{1,0:T(8,128)S(1)}, f32[7,128]{1,0:T(8,128)}, u32[]{:S(2)}) copy-start(f32[7,128]{1,0:T(8,128)} %get-tuple-element.605) | copy-start | bytes 10756
  437.1 8.1 %collective-permute-start.4 = (f32[2,1,128,128]{3,2,1,0:T(8,128)S(1)}, f32[2,1,128,128]{3,2,1,0:T(8,128)S(1)}, u32[]{:S(2)}, u32[]{:S(2)}) collective-permute-start(f32[2,1,128,128]{3,2,1,0:T(8,128)S(1)} %fusion.69), channel_id=1, source_target_pairs={{16,0},{32,16},{48,32},{64,48},{80,64},{96,80},{112,96},{128,112},... | collective-permute-start | bytes 393224 | tf_op jit(solution)/shard_map/ppermute | solution.py:17
  445.3 161.1 %copy-start.9 = (bf16[7,128,128]{1,2,0:T(8,128)(2,1)S(1)}, bf16[7,128,128]{1,2,0:T(8,128)(2,1)}, u32[]{:S(2)}) copy-start(bf16[7,128,128]{1,2,0:T(8,128)(2,1)} %get-tuple-element.505) | copy-start | bytes 688132
  445.3 7.6 %collective-permute-start.5 = (f32[2,1,128,128]{3,2,1,0:T(8,128)S(1)}, f32[2,1,128,128]{3,2,1,0:T(8,128)S(1)}, u32[]{:S(2)}, u32[]{:S(2)}) collective-permute-start(f32[2,1,128,128]{3,2,1,0:T(8,128)S(1)} %fusion.71), channel_id=1, source_target_pairs={{16,0},{32,16},{48,32},{64,48},{80,64},{96,80},{112,96},{128,112},... | collective-permute-start | bytes 393224 | tf_op jit(solution)/shard_map/ppermute | solution.py:17
  452.9 7.5 %collective-permute-start.6 = (f32[2,1,128,128]{3,2,1,0:T(8,128)S(1)}, f32[2,1,128,128]{3,2,1,0:T(8,128)S(1)}, u32[]{:S(2)}, u32[]{:S(2)}) collective-permute-start(f32[2,1,128,128]{3,2,1,0:T(8,128)S(1)} %fusion.65), channel_id=1, source_target_pairs={{16,0},{32,16},{48,32},{64,48},{80,64},{96,80},{112,96},{128,112},... | collective-permute-start | bytes 393224 | tf_op jit(solution)/shard_map/ppermute | solution.py:17
  460.4 146.8 %collective-permute-start.7 = (f32[2,1,128,128]{3,2,1,0:T(8,128)S(1)}, f32[2,1,128,128]{3,2,1,0:T(8,128)S(1)}, u32[]{:S(2)}, u32[]{:S(2)}) collective-permute-start(f32[2,1,128,128]{3,2,1,0:T(8,128)S(1)} %fusion.72), channel_id=1, source_target_pairs={{16,0},{32,16},{48,32},{64,48},{80,64},{96,80},{112,96},{128,112},... | collective-permute-start | bytes 393224 | tf_op jit(solution)/shard_map/ppermute | solution.py:17
Sparse Core Ops, SparseCore 0:
  76.7 97.0 all-gather.6
  215.6 94.0 all-gather.8
